TPU v7x, 256 devices: a whole 4x4x8 slice. The times are simulated.
256 devices in a mesh: seq: 16 (over x_hi, z), row: 4 (over x_lo, core), col: 4 (over y).
Axes of the slice: x: 4 (x_hi: 2, x_lo: 2; x = x_hi * 2 + x_lo), y: 4, z: 8, core: 2. Of those that a mesh axis runs over, the one named last changes fastest.
Arguments:
- tokens: bfloat16 [8192, 4096], P(('seq', 'col'), 'row'), may hold values from -11 to 11
- w_query: bfloat16 [4096, 4096], P('row', 'col'), as said below
- w_key: bfloat16 [4096, 1024], P('row', 'col'), as said below
- w_value: bfloat16 [4096, 1024], P('row', 'col'), may hold values from -0.09375 to 0.09375
- w_output: bfloat16 [4096, 4096], P('col', 'row'), may hold values from -0.09375 to 0.09375
Outputs:
- attended: bfloat16 [8192, 4096], P(('seq', 'col'), 'row')
Inputs may be any that keep to these rules, and one draw needn't show every extreme that they name: `w_query`: entries below 6 / sqrt(4096) in magnitude. `w_key`: entries below 8.4 / sqrt(4096) in magnitude.
All inputs are finite; a program needn't handle non-finite values.
Results may differ from a plain program's by a relative error of at most 0.025.
Values may be sent and summed in bfloat16 or wider, within the bound.
No kernel may reach another device: no remote copies, remote signals or barrier semaphores. Data moves between devices by JAX's collectives and lax.ppermute only.
A program may use at most 64 MiB of HBM per device.

v0:
```python
import jax
import jax.numpy as jnp
from jax import lax
from jax.sharding import PartitionSpec as P

HEADS = 32
KV_HEADS = 8
HEAD_DIM = 128
rope_base = 500000.0
masked_score = -1e30


def passed_along(value, axis, steps):
    count = lax.axis_size(axis)
    initial, last = (max(0, -steps), min(count, count - steps))
    return lax.ppermute(value, axis, [(source, source + steps) for source in range(initial, last)])


def rotate(values, positions):
    half = HEAD_DIM // 2
    freqs = rope_base ** (-(jnp.arange(half, dtype=jnp.float32) * 2.0) / HEAD_DIM)
    angles = positions.astype(jnp.float32)[:, None] * freqs[None, :]
    cosine = jnp.concatenate([jnp.cos(angles), jnp.cos(angles)], axis=1)
    sine = jnp.concatenate([jnp.sin(angles), jnp.sin(angles)], axis=1)
    count = values.shape[0]
    heads = values.reshape(count, -1, HEAD_DIM)
    turned = jnp.concatenate([-heads[..., half:], heads[..., :half]], axis=-1)
    result = heads * cosine[:, None, :] + turned * sine[:, None, :]
    return result.reshape(count, -1)


def on_device(tokens, w_query, w_key, w_value, w_output):
    shard_rows = tokens.shape[0]
    col_count = lax.axis_size("col")
    row_count = lax.axis_size("row")
    seq_count = lax.axis_size("seq")
    rows_dev = shard_rows * col_count // row_count
    block_len = rows_dev * row_count
    seq_at = lax.axis_index("seq")
    row_at = lax.axis_index("row")
    width_q = w_query.shape[1]
    width_kv = w_key.shape[1]
    local_kv = width_kv // HEAD_DIM
    group = HEADS // KV_HEADS
    score_scale = HEAD_DIM ** (-0.5)
    local_index = jnp.arange(block_len, dtype=jnp.int32)
    gathered_block = lax.all_gather(tokens, "col", axis=0, tiled=True)
    block_pos = seq_at * block_len + local_index
    regrouped = lax.all_to_all(gathered_block, "row", split_axis=0, concat_axis=1, tiled=True)
    projected = jnp.concatenate(
        [
            jnp.dot(
                regrouped,
                lax.all_gather(w_query, "row", axis=0, tiled=True),
                preferred_element_type=jnp.float32,
            ),
            jnp.dot(
                regrouped,
                lax.all_gather(w_key, "row", axis=0, tiled=True),
                preferred_element_type=jnp.float32,
            ),
            jnp.dot(
                regrouped,
                lax.all_gather(w_value, "row", axis=0, tiled=True),
                preferred_element_type=jnp.float32,
            ),
        ],
        axis=1,
    )
    q_pos = lax.dynamic_slice_in_dim(block_pos, row_at * rows_dev, rows_dev, 0)
    query = rotate(projected[:, :width_q], q_pos).astype(jnp.bfloat16)
    key_rot = rotate(projected[:, width_q : width_q + width_kv], q_pos)
    kv_slab = jnp.concatenate([key_rot, projected[:, width_q + width_kv :]], axis=1).astype(
        jnp.bfloat16
    )
    query_grouped = query.reshape(rows_dev, local_kv, group, HEAD_DIM)
    diagonal_mask = block_pos[None, :] <= q_pos[:, None]

    def attend(carry_state, queries, kv_rows, allowed):
        peak, total, summed = carry_state
        count = kv_rows.shape[0]
        key_blk = kv_rows[:, :width_kv].reshape(count, local_kv, HEAD_DIM)
        value_blk = kv_rows[:, width_kv:].reshape(count, local_kv, HEAD_DIM)
        scores = (
            jnp.einsum("qgha,kga->ghqk", queries, key_blk, preferred_element_type=jnp.float32)
            * score_scale
        )
        if allowed is not None:
            scores = jnp.where(allowed, scores, masked_score)
        new_peak = jnp.maximum(peak, jnp.max(scores, axis=-1))
        weights = jnp.exp(scores - new_peak[..., None])
        factor = jnp.exp(peak - new_peak)
        total = total * factor + jnp.sum(weights, axis=-1)
        summed = summed * factor[..., None] + jnp.einsum(
            "ghqk,kga->ghqa",
            weights.astype(jnp.bfloat16),
            value_blk,
            preferred_element_type=jnp.float32,
        )
        return (new_peak, total, summed)

    start_state = (
        jnp.full((local_kv, group, rows_dev), masked_score, jnp.float32),
        jnp.zeros((local_kv, group, rows_dev), jnp.float32),
        jnp.zeros((local_kv, group, rows_dev, HEAD_DIM), jnp.float32),
    )

    def keep_state(carry_state):
        return carry_state

    def cycle_work(step_index, carry_state, kv_whole):
        source_dev = (seq_at - step_index) % seq_count
        return lax.cond(
            source_dev < seq_at,
            lambda inner: attend(inner, query_grouped, kv_whole, None),
            keep_state,
            carry_state,
        )

    kv_first = lax.all_gather(kv_slab, "row", axis=0, tiled=True)
    first_state = attend(start_state, query_grouped, kv_first, diagonal_mask)

    def cycle_turn(step_index, carry):
        carry_state, kv_here = carry
        kv_here = passed_along(kv_here, "seq", 1)
        return (cycle_work(step_index, carry_state, kv_here), kv_here)

    final_state, _ = lax.fori_loop(1, seq_count, cycle_turn, (first_state, kv_first))
    heads_sum = final_state[2] / final_state[1][..., None]
    heads_out = heads_sum.transpose(2, 0, 1, 3).reshape(rows_dev, width_q).astype(jnp.bfloat16)
    heads_block = lax.all_gather(heads_out, "row", axis=0, tiled=True)
    return lax.psum_scatter(
        jnp.dot(heads_block, w_output, preferred_element_type=jnp.float32).astype(jnp.bfloat16),
        "col",
        scatter_dimension=0,
        tiled=True,
    )


def solution(mesh):
    return jax.shard_map(
        on_device,
        mesh=mesh,
        in_specs=(
            P(("seq", "col"), "row"),
            P("row", "col"),
            P("row", "col"),
            P("row", "col"),
            P("col", "row"),
        ),
        out_specs=P(("seq", "col"), "row"),
        check_vma=False,
    )
```

profile of v0, /device:TPU:2, one launch (start us, length us, event | category | flops | bytes accessed | tf_op | source)
XLA Modules:
  0.0 549.9 jit_solution(10497414819965394275)
XLA Ops:
  9.3 29.5 %all-gather.6.cloned.1.call-done = bf16[512,1024]{1,0:T(8,128)(2,1)} async-done(((bf16[128,1024]{1,0:T(8,128)(2,1)}), bf16[512,1024]{1,0:T(8,128)(2,1)}) %all-gather.6.cloned.1.call-update) | async-done | bytes 1048592 | tf_op jit(solution)/shard_map/all_gather | solution.py:47
  38.8 4.0 all-to-all-start
  43.9 12.4 %all-to-all-done = bf16[4,128,1024]{2,1,0:T(8,128)(2,1)S(1)} async-done(((bf16[4,128,1024]{2,1,0:T(8,128)(2,1)}), bf16[4,128,1024]{2,1,0:T(8,128)(2,1)S(1)}, u32[]{:S(2)}, u32[]{:S(2)}) %all-to-all-start) | async-done | bytes 1048608 | tf_op jit(solution)/shard_map/all_to_all | solution.py:49
  61.0 2.4 copy.59
  63.3 9.0 %all-gather.8.cloned.1.call-done = bf16[4096,256]{1,0:T(8,128)(2,1)} async-done(((bf16[1024,256]{1,0:T(8,128)(2,1)}), bf16[4096,256]{1,0:T(8,128)(2,1)}) %all-gather.8.cloned.1.call-update) | async-done | bytes 2097168 | tf_op jit(solution)/shard_map/all_gather | solution.py:59
  72.3 4.1 copy.34
  76.4 2.3 fusion.22
  78.9 26.6 %all-gather.10.cloned.1.call-done = bf16[4096,256]{1,0:T(8,128)(2,1)} async-done(((bf16[1024,256]{1,0:T(8,128)(2,1)}), bf16[4096,256]{1,0:T(8,128)(2,1)}) %all-gather.10.cloned.1.call-update) | async-done | bytes 2097168 | tf_op jit(solution)/shard_map/all_gather | solution.py:64
  105.5 2.4 convolution_convert_fusion.1
  107.9 8.2 %all_gather.21 = bf16[512,512]{1,0:T(8,128)(2,1)} all-gather(bf16[128,512]{1,0:T(8,128)(2,1)S(1)} %pad_maximum_fusion), channel_id=1, replica_groups=mesh['seq'=16,'row'=4,'col'=4] {'row'}, dimensions={0}, use_global_device_ids=true | all-gather | bytes 655360 | tf_op jit(solution)/shard_map/all_gather | solution.py:120
  116.1 2.0 copy.41
  122.4 69.7 %all-gather.12.cloned.1.call-done = bf16[4096,1024]{1,0:T(8,128)(2,1)} async-done(((bf16[1024,1024]{1,0:T(8,128)(2,1)}), bf16[4096,1024]{1,0:T(8,128)(2,1)}) %all-gather.12.cloned.1.call-update) | async-done | bytes 8388624 | tf_op jit(solution)/shard_map/all_gather | solution.py:54
  192.1 11.6 %copy.36 = bf16[1024,4096]{1,0:T(8,128)(2,1)} copy(bf16[1024,4096]{0,1:T(8,128)(2,1)} %bitcast.60) | data formatting | bytes 16777216 | tf_op jit(solution)/shard_map/dot_general | solution.py:52
  203.7 5.7 %fusion.23 = f32[128,8,128]{0,2,1:T(8,128)S(1)} fusion(bf16[128,4096,1]{1,0,2:T(8,128)(2,1)S(1)} %reshape.59, bf16[8,128,4096]{2,1,0:T(8,128)(2,1)} %bitcast.55), kind=kOutput, calls=%fused_computation.46 | convolution fusion | flops 1073741824 | bytes 9961472 | tf_op jit(solution)/shard_map/dot_general | solution.py:52
  211.9 231.9 %while.21 = (s32[]{:T(128)}, f32[2,4,128]{2,1,0:T(4,128)S(1)}, f32[2,4,128]{2,1,0:T(4,128)S(1)}, f32[2,4,128,128]{3,2,1,0:T(8,128)S(1)}, bf16[512,512]{0,1:T(8,1...) while((s32[]{:T(128)}, f32[2,4,128]{2,1,0:T(4,128)S(1)}, ...), condition=%wide.region_7.8_spmd, body=%wide.region_2.7_spmd.sunk | while | flops 272893952 | bytes 12386684 | solution.py:128
  212.0 3.5 collective-permute-start
  215.5 12.5 %collective-permute-done = bf16[512,512]{0,1:T(8,128)(2,1)S(1)} collective-permute-done((bf16[512,512]{0,1:T(8,128)(2,1)}, bf16[512,512]{0,1:T(8,128)(2,1)S(1)}, u32[]{:S(2)}, u32[]{:S(2)}) %collective-permute-start) | collective-permute-done | bytes 524320 | tf_op jit(solution)/shard_map/while/body/eval_jaxpr/ppermute | solution.py:16
  228.8 6.0 %collective-permute-start = (bf16[512,512]{0,1:T(8,128)(2,1)}, bf16[512,512]{0,1:T(8,128)(2,1)S(1)}, u32[]{:S(2)}, u32[]{:S(2)}) collective-permute-start(bf16[512,512]{0,1:T(8,128)(2,1)} %get-tuple-element.353), channel_id=1, source_target_pairs={{0,16},{16,32},{32,48},{48,64},{64,80},{80,96},{96,112},{112,128},... | collective-permute-start | bytes 1572872 | tf_op jit(solution)/shard_map/while/body/eval_jaxpr/ppermute | solution.py:16
  234.8 11.7 %collective-permute-done = bf16[512,512]{0,1:T(8,128)(2,1)S(1)} collective-permute-done((bf16[512,512]{0,1:T(8,128)(2,1)}, bf16[512,512]{0,1:T(8,128)(2,1)S(1)}, u32[]{:S(2)}, u32[]{:S(2)}) %collective-permute-start) | collective-permute-done | bytes 524320 | tf_op jit(solution)/shard_map/while/body/eval_jaxpr/ppermute | solution.py:16
  247.3 4.3 collective-permute-start
  251.6 10.9 %collective-permute-done = bf16[512,512]{0,1:T(8,128)(2,1)S(1)} collective-permute-done((bf16[512,512]{0,1:T(8,128)(2,1)}, bf16[512,512]{0,1:T(8,128)(2,1)S(1)}, u32[]{:S(2)}, u32[]{:S(2)}) %collective-permute-start) | collective-permute-done | bytes 524320 | tf_op jit(solution)/shard_map/while/body/eval_jaxpr/ppermute | solution.py:16
  263.3 5.2 collective-permute-start
  268.5 10.0 %collective-permute-done = bf16[512,512]{0,1:T(8,128)(2,1)S(1)} collective-permute-done((bf16[512,512]{0,1:T(8,128)(2,1)}, bf16[512,512]{0,1:T(8,128)(2,1)S(1)}, u32[]{:S(2)}, u32[]{:S(2)}) %collective-permute-start) | collective-permute-done | bytes 524320 | tf_op jit(solution)/shard_map/while/body/eval_jaxpr/ppermute | solution.py:16
  279.3 5.1 collective-permute-start
  284.4 9.1 %collective-permute-done = bf16[512,512]{0,1:T(8,128)(2,1)S(1)} collective-permute-done((bf16[512,512]{0,1:T(8,128)(2,1)}, bf16[512,512]{0,1:T(8,128)(2,1)S(1)}, u32[]{:S(2)}, u32[]{:S(2)}) %collective-permute-start) | collective-permute-done | bytes 524320 | tf_op jit(solution)/shard_map/while/body/eval_jaxpr/ppermute | solution.py:16
  294.3 7.2 %collective-permute-start = (bf16[512,512]{0,1:T(8,128)(2,1)}, bf16[512,512]{0,1:T(8,128)(2,1)S(1)}, u32[]{:S(2)}, u32[]{:S(2)}) collective-permute-start(bf16[512,512]{0,1:T(8,128)(2,1)} %get-tuple-element.353), channel_id=1, source_target_pairs={{0,16},{16,32},{32,48},{48,64},{64,80},{80,96},{96,112},{112,128},... | collective-permute-start | bytes 1572872 | tf_op jit(solution)/shard_map/while/body/eval_jaxpr/ppermute | solution.py:16
  301.6 8.3 %collective-permute-done = bf16[512,512]{0,1:T(8,128)(2,1)S(1)} collective-permute-done((bf16[512,512]{0,1:T(8,128)(2,1)}, bf16[512,512]{0,1:T(8,128)(2,1)S(1)}, u32[]{:S(2)}, u32[]{:S(2)}) %collective-permute-start) | collective-permute-done | bytes 524320 | tf_op jit(solution)/shard_map/while/body/eval_jaxpr/ppermute | solution.py:16
  310.6 5.5 %collective-permute-start = (bf16[512,512]{0,1:T(8,128)(2,1)}, bf16[512,512]{0,1:T(8,128)(2,1)S(1)}, u32[]{:S(2)}, u32[]{:S(2)}) collective-permute-start(bf16[512,512]{0,1:T(8,128)(2,1)} %get-tuple-element.353), channel_id=1, source_target_pairs={{0,16},{16,32},{32,48},{48,64},{64,80},{80,96},{96,112},{112,128},... | collective-permute-start | bytes 1572872 | tf_op jit(solution)/shard_map/while/body/eval_jaxpr/ppermute | solution.py:16
  316.2 7.4 %collective-permute-done = bf16[512,512]{0,1:T(8,128)(2,1)S(1)} collective-permute-done((bf16[512,512]{0,1:T(8,128)(2,1)}, bf16[512,512]{0,1:T(8,128)(2,1)S(1)}, u32[]{:S(2)}, u32[]{:S(2)}) %collective-permute-start) | collective-permute-done | bytes 524320 | tf_op jit(solution)/shard_map/while/body/eval_jaxpr/ppermute | solution.py:16
  324.4 7.2 %collective-permute-start = (bf16[512,512]{0,1:T(8,128)(2,1)}, bf16[512,512]{0,1:T(8,128)(2,1)S(1)}, u32[]{:S(2)}, u32[]{:S(2)}) collective-permute-start(bf16[512,512]{0,1:T(8,128)(2,1)} %get-tuple-element.353), channel_id=1, source_target_pairs={{0,16},{16,32},{32,48},{48,64},{64,80},{80,96},{96,112},{112,128},... | collective-permute-start | bytes 1572872 | tf_op jit(solution)/shard_map/while/body/eval_jaxpr/ppermute | solution.py:16
  331.7 6.9 %collective-permute-done = bf16[512,512]{0,1:T(8,128)(2,1)S(1)} collective-permute-done((bf16[512,512]{0,1:T(8,128)(2,1)}, bf16[512,512]{0,1:T(8,128)(2,1)S(1)}, u32[]{:S(2)}, u32[]{:S(2)}) %collective-permute-start) | collective-permute-done | bytes 524320 | tf_op jit(solution)/shard_map/while/body/eval_jaxpr/ppermute | solution.py:16
  339.4 5.5 %collective-permute-start = (bf16[512,512]{0,1:T(8,128)(2,1)}, bf16[512,512]{0,1:T(8,128)(2,1)S(1)}, u32[]{:S(2)}, u32[]{:S(2)}) collective-permute-start(bf16[512,512]{0,1:T(8,128)(2,1)} %get-tuple-element.353), channel_id=1, source_target_pairs={{0,16},{16,32},{32,48},{48,64},{64,80},{80,96},{96,112},{112,128},... | collective-permute-start | bytes 1572872 | tf_op jit(solution)/shard_map/while/body/eval_jaxpr/ppermute | solution.py:16
  345.0 7.0 %collective-permute-done = bf16[512,512]{0,1:T(8,128)(2,1)S(1)} collective-permute-done((bf16[512,512]{0,1:T(8,128)(2,1)}, bf16[512,512]{0,1:T(8,128)(2,1)S(1)}, u32[]{:S(2)}, u32[]{:S(2)}) %collective-permute-start) | collective-permute-done | bytes 524320 | tf_op jit(solution)/shard_map/while/body/eval_jaxpr/ppermute | solution.py:16
  352.7 5.5 %collective-permute-start = (bf16[512,512]{0,1:T(8,128)(2,1)}, bf16[512,512]{0,1:T(8,128)(2,1)S(1)}, u32[]{:S(2)}, u32[]{:S(2)}) collective-permute-start(bf16[512,512]{0,1:T(8,128)(2,1)} %get-tuple-element.353), channel_id=1, source_target_pairs={{0,16},{16,32},{32,48},{48,64},{64,80},{80,96},{96,112},{112,128},... | collective-permute-start | bytes 1572872 | tf_op jit(solution)/shard_map/while/body/eval_jaxpr/ppermute | solution.py:16
  358.3 7.8 %collective-permute-done = bf16[512,512]{0,1:T(8,128)(2,1)S(1)} collective-permute-done((bf16[512,512]{0,1:T(8,128)(2,1)}, bf16[512,512]{0,1:T(8,128)(2,1)S(1)}, u32[]{:S(2)}, u32[]{:S(2)}) %collective-permute-start) | collective-permute-done | bytes 524320 | tf_op jit(solution)/shard_map/while/body/eval_jaxpr/ppermute | solution.py:16
  366.9 4.6 collective-permute-start
  371.5 6.9 %collective-permute-done = bf16[512,512]{0,1:T(8,128)(2,1)S(1)} collective-permute-done((bf16[512,512]{0,1:T(8,128)(2,1)}, bf16[512,512]{0,1:T(8,128)(2,1)S(1)}, u32[]{:S(2)}, u32[]{:S(2)}) %collective-permute-start) | collective-permute-done | bytes 524320 | tf_op jit(solution)/shard_map/while/body/eval_jaxpr/ppermute | solution.py:16
  379.3 7.7 %collective-permute-start = (bf16[512,512]{0,1:T(8,128)(2,1)}, bf16[512,512]{0,1:T(8,128)(2,1)S(1)}, u32[]{:S(2)}, u32[]{:S(2)}) collective-permute-start(bf16[512,512]{0,1:T(8,128)(2,1)} %get-tuple-element.353), channel_id=1, source_target_pairs={{0,16},{16,32},{32,48},{48,64},{64,80},{80,96},{96,112},{112,128},... | collective-permute-start | bytes 1572872 | tf_op jit(solution)/shard_map/while/body/eval_jaxpr/ppermute | solution.py:16
  387.0 7.1 %collective-permute-done = bf16[512,512]{0,1:T(8,128)(2,1)S(1)} collective-permute-done((bf16[512,512]{0,1:T(8,128)(2,1)}, bf16[512,512]{0,1:T(8,128)(2,1)S(1)}, u32[]{:S(2)}, u32[]{:S(2)}) %collective-permute-start) | collective-permute-done | bytes 524320 | tf_op jit(solution)/shard_map/while/body/eval_jaxpr/ppermute | solution.py:16
  394.9 7.7 %collective-permute-start = (bf16[512,512]{0,1:T(8,128)(2,1)}, bf16[512,512]{0,1:T(8,128)(2,1)S(1)}, u32[]{:S(2)}, u32[]{:S(2)}) collective-permute-start(bf16[512,512]{0,1:T(8,128)(2,1)} %get-tuple-element.353), channel_id=1, source_target_pairs={{0,16},{16,32},{32,48},{48,64},{64,80},{80,96},{96,112},{112,128},... | collective-permute-start | bytes 1572872 | tf_op jit(solution)/shard_map/while/body/eval_jaxpr/ppermute | solution.py:16
  402.6 6.9 %collective-permute-done = bf16[512,512]{0,1:T(8,128)(2,1)S(1)} collective-permute-done((bf16[512,512]{0,1:T(8,128)(2,1)}, bf16[512,512]{0,1:T(8,128)(2,1)S(1)}, u32[]{:S(2)}, u32[]{:S(2)}) %collective-permute-start) | collective-permute-done | bytes 524320 | tf_op jit(solution)/shard_map/while/body/eval_jaxpr/ppermute | solution.py:16
  410.4 10.7 %collective-permute-start = (bf16[512,512]{0,1:T(8,128)(2,1)}, bf16[512,512]{0,1:T(8,128)(2,1)S(1)}, u32[]{:S(2)}, u32[]{:S(2)}) collective-permute-start(bf16[512,512]{0,1:T(8,128)(2,1)} %get-tuple-element.353), channel_id=1, source_target_pairs={{0,16},{16,32},{32,48},{48,64},{64,80},{80,96},{96,112},{112,128},... | collective-permute-start | bytes 1572872 | tf_op jit(solution)/shard_map/while/body/eval_jaxpr/ppermute | solution.py:16
  421.1 8.8 %collective-permute-done = bf16[512,512]{0,1:T(8,128)(2,1)S(1)} collective-permute-done((bf16[512,512]{0,1:T(8,128)(2,1)}, bf16[512,512]{0,1:T(8,128)(2,1)S(1)}, u32[]{:S(2)}, u32[]{:S(2)}) %collective-permute-start) | collective-permute-done | bytes 524320 | tf_op jit(solution)/shard_map/while/body/eval_jaxpr/ppermute | solution.py:16
  430.7 5.4 collective-permute-start
  436.1 6.9 %collective-permute-done = bf16[512,512]{0,1:T(8,128)(2,1)S(1)} collective-permute-done((bf16[512,512]{0,1:T(8,128)(2,1)}, bf16[512,512]{0,1:T(8,128)(2,1)S(1)}, u32[]{:S(2)}, u32[]{:S(2)}) %collective-permute-start) | collective-permute-done | bytes 524320 | tf_op jit(solution)/shard_map/while/body/eval_jaxpr/ppermute | solution.py:16
  444.9 66.5 %all-gather.14.cloned.1.call-done = bf16[512,1024]{0,1:T(8,128)(2,1)} async-done(((bf16[128,1024]{0,1:T(8,128)(2,1)}), bf16[512,1024]{0,1:T(8,128)(2,1)}) %all-gather.14.cloned.1.call-update) | async-done | bytes 1048592 | tf_op jit(solution)/shard_map/all_gather | solution.py:131
  511.4 3.5 convolution_convert_fusion
  514.9 28.2 %reduce-scatter.2.cloned.1.call-done = bf16[128,1024]{1,0:T(8,128)(2,1)} async-done(((bf16[512,1024]{1,0:T(8,128)(2,1)}), bf16[128,1024]{1,0:T(8,128)(2,1)}) %reduce-scatter.2.cloned.1.call-update) | async-done | bytes 262160 | tf_op jit(solution)/shard_map/reduce_scatter | solution.py:132
  (77 shorter events, 28.3 us)
Async XLA Ops:
  6.5 504.9 %copy-start = (bf16[1024,1024]{1,0:T(8,128)(2,1)S(1)}, bf16[1024,1024]{1,0:T(8,128)(2,1)}, u32[]{:S(2)}) copy-start(bf16[1024,1024]{1,0:T(8,128)(2,1)} %param.13) | copy-start | bytes 6291460
  6.5 32.3 %all-gather.6.cloned.1.call-start = ((), (), s32[]{:S(2)}) async-start(), calls=%async_computation.2 | async-start | bytes 1310720 | tf_op jit(solution)/shard_map/all_gather | solution.py:47
  7.3 65.1 %all-gather.8.cloned.1.call-start = ((), (), s32[]{:S(2)}) async-start(), calls=%async_computation.3 | async-start | bytes 2621440 | tf_op jit(solution)/shard_map/all_gather | solution.py:59
  8.0 97.5 %all-gather.10.cloned.1.call-start = ((), (), s32[]{:S(2)}) async-start(), calls=%async_computation.4 | async-start | bytes 2621440 | tf_op jit(solution)/shard_map/all_gather | solution.py:64
  8.7 183.3 %all-gather.12.cloned.1.call-start = ((), (), s32[]{:S(2)}) async-start(), calls=%async_computation.5 | async-start | bytes 10485760 | tf_op jit(solution)/shard_map/all_gather | solution.py:54
  38.8 17.5 %all-to-all-start = ((bf16[4,128,1024]{2,1,0:T(8,128)(2,1)}), bf16[4,128,1024]{2,1,0:T(8,128)(2,1)S(1)}, u32[]{:S(2)}, u32[]{:S(2)}) async-start(bf16[4,128,1024]{2,1,0:T(8,128)(2,1)} %bitcast.68), calls=%async_computation | async-start | bytes 2097152 | tf_op jit(solution)/shard_map/all_to_all | solution.py:49
  42.8 468.5 %all-gather.14.cloned.1.call-start = ((), (), s32[]{:S(2)}) async-start(), calls=%async_computation.6 | async-start | bytes 1310720 | tf_op jit(solution)/shard_map/all_gather | solution.py:131
  56.3 1.0 copy-start.1
  209.4 1.0 copy-start.3
  209.4 0.9 copy-start.4
  210.3 1.0 copy-start.2
  212.0 16.0 %collective-permute-start = (bf16[512,512]{0,1:T(8,128)(2,1)}, bf16[512,512]{0,1:T(8,128)(2,1)S(1)}, u32[]{:S(2)}, u32[]{:S(2)}) collective-permute-start(bf16[512,512]{0,1:T(8,128)(2,1)} %get-tuple-element.353), channel_id=1, source_target_pairs={{0,16},{16,32},{32,48},{48,64},{64,80},{80,96},{96,112},{112,128},... | collective-permute-start | bytes 1572872 | tf_op jit(solution)/shard_map/while/body/eval_jaxpr/ppermute | solution.py:16
  228.8 17.7 %collective-permute-start = (bf16[512,512]{0,1:T(8,128)(2,1)}, bf16[512,512]{0,1:T(8,128)(2,1)S(1)}, u32[]{:S(2)}, u32[]{:S(2)}) collective-permute-start(bf16[512,512]{0,1:T(8,128)(2,1)} %get-tuple-element.353), channel_id=1, source_target_pairs={{0,16},{16,32},{32,48},{48,64},{64,80},{80,96},{96,112},{112,128},... | collective-permute-start | bytes 1572872 | tf_op jit(solution)/shard_map/while/body/eval_jaxpr/ppermute | solution.py:16
  247.3 15.2 %collective-permute-start = (bf16[512,512]{0,1:T(8,128)(2,1)}, bf16[512,512]{0,1:T(8,128)(2,1)S(1)}, u32[]{:S(2)}, u32[]{:S(2)}) collective-permute-start(bf16[512,512]{0,1:T(8,128)(2,1)} %get-tuple-element.353), channel_id=1, source_target_pairs={{0,16},{16,32},{32,48},{48,64},{64,80},{80,96},{96,112},{112,128},... | collective-permute-start | bytes 1572872 | tf_op jit(solution)/shard_map/while/body/eval_jaxpr/ppermute | solution.py:16
  263.3 15.2 %collective-permute-start = (bf16[512,512]{0,1:T(8,128)(2,1)}, bf16[512,512]{0,1:T(8,128)(2,1)S(1)}, u32[]{:S(2)}, u32[]{:S(2)}) collective-permute-start(bf16[512,512]{0,1:T(8,128)(2,1)} %get-tuple-element.353), channel_id=1, source_target_pairs={{0,16},{16,32},{32,48},{48,64},{64,80},{80,96},{96,112},{112,128},... | collective-permute-start | bytes 1572872 | tf_op jit(solution)/shard_map/while/body/eval_jaxpr/ppermute | solution.py:16
  279.3 14.3 %collective-permute-start = (bf16[512,512]{0,1:T(8,128)(2,1)}, bf16[512,512]{0,1:T(8,128)(2,1)S(1)}, u32[]{:S(2)}, u32[]{:S(2)}) collective-permute-start(bf16[512,512]{0,1:T(8,128)(2,1)} %get-tuple-element.353), channel_id=1, source_target_pairs={{0,16},{16,32},{32,48},{48,64},{64,80},{80,96},{96,112},{112,128},... | collective-permute-start | bytes 1572872 | tf_op jit(solution)/shard_map/while/body/eval_jaxpr/ppermute | solution.py:16
  294.3 15.5 %collective-permute-start = (bf16[512,512]{0,1:T(8,128)(2,1)}, bf16[512,512]{0,1:T(8,128)(2,1)S(1)}, u32[]{:S(2)}, u32[]{:S(2)}) collective-permute-start(bf16[512,512]{0,1:T(8,128)(2,1)} %get-tuple-element.353), channel_id=1, source_target_pairs={{0,16},{16,32},{32,48},{48,64},{64,80},{80,96},{96,112},{112,128},... | collective-permute-start | bytes 1572872 | tf_op jit(solution)/shard_map/while/body/eval_jaxpr/ppermute | solution.py:16
  310.6 13.0 %collective-permute-start = (bf16[512,512]{0,1:T(8,128)(2,1)}, bf16[512,512]{0,1:T(8,128)(2,1)S(1)}, u32[]{:S(2)}, u32[]{:S(2)}) collective-permute-start(bf16[512,512]{0,1:T(8,128)(2,1)} %get-tuple-element.353), channel_id=1, source_target_pairs={{0,16},{16,32},{32,48},{48,64},{64,80},{80,96},{96,112},{112,128},... | collective-permute-start | bytes 1572872 | tf_op jit(solution)/shard_map/while/body/eval_jaxpr/ppermute | solution.py:16
  324.4 14.2 %collective-permute-start = (bf16[512,512]{0,1:T(8,128)(2,1)}, bf16[512,512]{0,1:T(8,128)(2,1)S(1)}, u32[]{:S(2)}, u32[]{:S(2)}) collective-permute-start(bf16[512,512]{0,1:T(8,128)(2,1)} %get-tuple-element.353), channel_id=1, source_target_pairs={{0,16},{16,32},{32,48},{48,64},{64,80},{80,96},{96,112},{112,128},... | collective-permute-start | bytes 1572872 | tf_op jit(solution)/shard_map/while/body/eval_jaxpr/ppermute | solution.py:16
  339.4 12.5 %collective-permute-start = (bf16[512,512]{0,1:T(8,128)(2,1)}, bf16[512,512]{0,1:T(8,128)(2,1)S(1)}, u32[]{:S(2)}, u32[]{:S(2)}) collective-permute-start(bf16[512,512]{0,1:T(8,128)(2,1)} %get-tuple-element.353), channel_id=1, source_target_pairs={{0,16},{16,32},{32,48},{48,64},{64,80},{80,96},{96,112},{112,128},... | collective-permute-start | bytes 1572872 | tf_op jit(solution)/shard_map/while/body/eval_jaxpr/ppermute | solution.py:16
  352.7 13.4 %collective-permute-start = (bf16[512,512]{0,1:T(8,128)(2,1)}, bf16[512,512]{0,1:T(8,128)(2,1)S(1)}, u32[]{:S(2)}, u32[]{:S(2)}) collective-permute-start(bf16[512,512]{0,1:T(8,128)(2,1)} %get-tuple-element.353), channel_id=1, source_target_pairs={{0,16},{16,32},{32,48},{48,64},{64,80},{80,96},{96,112},{112,128},... | collective-permute-start | bytes 1572872 | tf_op jit(solution)/shard_map/while/body/eval_jaxpr/ppermute | solution.py:16
  366.9 11.6 %collective-permute-start = (bf16[512,512]{0,1:T(8,128)(2,1)}, bf16[512,512]{0,1:T(8,128)(2,1)S(1)}, u32[]{:S(2)}, u32[]{:S(2)}) collective-permute-start(bf16[512,512]{0,1:T(8,128)(2,1)} %get-tuple-element.353), channel_id=1, source_target_pairs={{0,16},{16,32},{32,48},{48,64},{64,80},{80,96},{96,112},{112,128},... | collective-permute-start | bytes 1572872 | tf_op jit(solution)/shard_map/while/body/eval_jaxpr/ppermute | solution.py:16
  379.3 14.8 %collective-permute-start = (bf16[512,512]{0,1:T(8,128)(2,1)}, bf16[512,512]{0,1:T(8,128)(2,1)S(1)}, u32[]{:S(2)}, u32[]{:S(2)}) collective-permute-start(bf16[512,512]{0,1:T(8,128)(2,1)} %get-tuple-element.353), channel_id=1, source_target_pairs={{0,16},{16,32},{32,48},{48,64},{64,80},{80,96},{96,112},{112,128},... | collective-permute-start | bytes 1572872 | tf_op jit(solution)/shard_map/while/body/eval_jaxpr/ppermute | solution.py:16
  394.9 14.7 %collective-permute-start = (bf16[512,512]{0,1:T(8,128)(2,1)}, bf16[512,512]{0,1:T(8,128)(2,1)S(1)}, u32[]{:S(2)}, u32[]{:S(2)}) collective-permute-start(bf16[512,512]{0,1:T(8,128)(2,1)} %get-tuple-element.353), channel_id=1, source_target_pairs={{0,16},{16,32},{32,48},{48,64},{64,80},{80,96},{96,112},{112,128},... | collective-permute-start | bytes 1572872 | tf_op jit(solution)/shard_map/while/body/eval_jaxpr/ppermute | solution.py:16
  410.4 19.5 %collective-permute-start = (bf16[512,512]{0,1:T(8,128)(2,1)}, bf16[512,512]{0,1:T(8,128)(2,1)S(1)}, u32[]{:S(2)}, u32[]{:S(2)}) collective-permute-start(bf16[512,512]{0,1:T(8,128)(2,1)} %get-tuple-element.353), channel_id=1, source_target_pairs={{0,16},{16,32},{32,48},{48,64},{64,80},{80,96},{96,112},{112,128},... | collective-permute-start | bytes 1572872 | tf_op jit(solution)/shard_map/while/body/eval_jaxpr/ppermute | solution.py:16
  430.7 12.4 %collective-permute-start = (bf16[512,512]{0,1:T(8,128)(2,1)}, bf16[512,512]{0,1:T(8,128)(2,1)S(1)}, u32[]{:S(2)}, u32[]{:S(2)}) collective-permute-start(bf16[512,512]{0,1:T(8,128)(2,1)} %get-tuple-element.353), channel_id=1, source_target_pairs={{0,16},{16,32},{32,48},{48,64},{64,80},{80,96},{96,112},{112,128},... | collective-permute-start | bytes 1572872 | tf_op jit(solution)/shard_map/while/body/eval_jaxpr/ppermute | solution.py:16
  444.9 98.2 %reduce-scatter.2.cloned.1.call-start = ((), (), s32[]{:S(2)}) async-start(), calls=%async_computation.7 | async-start | bytes 1310720 | tf_op jit(solution)/shard_map/reduce_scatter | solution.py:132
Sparse Core Ops, SparseCore 0:
  9.1 29.6 all-gather.5
  40.6 31.6 all-gather.7
  74.1 31.3 all-gather.9
  107.2 84.8 all-gather.11
  445.0 66.3 all-gather.13
  515.0 28.0 reduce-scatter.1
where the time goes:
time: 551 us; the launch traced here: 550 us
  waiting for transfers between devices  373 us (68%)
  starting transfers between devices  95.4 us (17%)
  local copies, waits for them, and re-layouts  42.2 us (8%)
  matrix products  14.9 us (3%)
  between operations  13.6 us (2%)
  blocking collectives  8.21 us (1%)
    ppermute x15, waiting for transfers between devices, passed_along(): lax.ppermute(value, axis, [(source, source + steps) for source in range(i...  128 us
    ppermute x15, starting transfers between devices, passed_along(): lax.ppermute(value, axis, [(source, source + steps) for source in range(i...  91.2 us
    all_gather x1, waiting for transfers between devices, on_device(): lax.all_gather(w_query, 'row', axis=0, tiled=True)  69.7 us
    all_gather x1, waiting for transfers between devices, on_device(): heads_block = lax.all_gather(heads_out, 'row', axis=0, tiled=True)  66.5 us
    all_gather x1, waiting for transfers between devices, on_device(): gathered_block = lax.all_gather(tokens, 'col', axis=0, tiled=True)  29.5 us
    reduce_scatter x1, waiting for transfers between devices, on_device(): lax.psum_scatter(jnp.dot(heads_block, w_output, preferred_element_type=jn...  28.2 us
    all_gather x1, waiting for transfers between devices, on_device(): lax.all_gather(w_value, 'row', axis=0, tiled=True)  26.6 us
    all_to_all x1, waiting for transfers between devices, on_device(): lax.all_to_all(gathered_block, 'row', split_axis=0, concat_axis=1, tiled=...  12.4 us
  transfers between devices with their start and end apart: 22, of which 22 were waited for; matrix products, arithmetic and copies ran while one was open for 4% of the time, Pallas kernels for 0%

commit v1 on v0

--- a/solution.py
+++ b/solution.py
@@ -1,3 +1,4 @@
+import functools
 import jax
 import jax.numpy as jnp
 from jax import lax
@@ -8,6 +9,39 @@
 HEAD_DIM = 128
 rope_base = 500000.0
 masked_score = -1e30
+
+
+def spot_connect(buf, array_axis):
+    buf = jnp.moveaxis(buf, 0, array_axis)
+    parts_out = buf.shape
+    return buf.reshape(
+        *parts_out[:array_axis],
+        parts_out[array_axis] * parts_out[array_axis + 1],
+        *parts_out[array_axis + 2 :]
+    )
+
+
+def trace_slabs(payload, along_axis, array_dim):
+    n_shards = lax.axis_size(along_axis)
+    pile = [(jj, (jj + 1) % n_shards) for jj in range(n_shards)]
+    newest, piece_next = ([], [])
+    store = [(num, j) for j, num in pile]
+    for k in range(n_shards - 1):
+        if k % 2 == 0:
+            block_next = lax.ppermute(newest[-1] if newest else payload, along_axis, pile)
+            newest.append(block_next)
+        else:
+            k_now = lax.ppermute(piece_next[-1] if piece_next else payload, along_axis, store)
+            piece_next.append(k_now)
+    later = jnp.stack([*newest[::-1], payload, *piece_next])
+    near = lax.axis_index(along_axis)
+    spare = len(newest)
+    then = near - spare
+    later = later[(jnp.arange(n_shards) - then) % n_shards]
+    return spot_connect(later, array_dim)
+
+
+deliver_shapes = functools.partial(trace_slabs, along_axis="col", array_dim=0)
 
 
 def passed_along(value, axis, steps):
@@ -44,7 +78,7 @@
     group = HEADS // KV_HEADS
     score_scale = HEAD_DIM ** (-0.5)
     local_index = jnp.arange(block_len, dtype=jnp.int32)
-    gathered_block = lax.all_gather(tokens, "col", axis=0, tiled=True)
+    gathered_block = deliver_shapes(tokens)
     block_pos = seq_at * block_len + local_index
     regrouped = lax.all_to_all(gathered_block, "row", split_axis=0, concat_axis=1, tiled=True)
     projected = jnp.concatenate(

time: 551 us -> 530 us (0.962)
  waiting for transfers between devices: 373 us -> 344 us
    all_gather x1 -> x0, waiting for transfers between devices: 29.5 us -> none  [on_device(): gathered_block = lax.all_gather(tokens, 'col', axis=0, tiled=True)]
    ppermute x0 -> x3, waiting for transfers between devices: none -> 14.2 us  [the longest x2 14.2 us: trace_slabs(): lax.ppermute(newest[-1] if newest else payload, along_axis, pile)]
    all_gather x1, waiting for transfers between devices: 26.6 us -> 16.8 us  [on_device(): lax.all_gather(w_value, 'row', axis=0, tiled=True)]
    all_gather x1, waiting for transfers between devices: 8.99 us -> 0.01 us  [on_device(): lax.all_gather(w_key, 'row', axis=0, tiled=True)]
    all_to_all x1, waiting for transfers between devices: 12.4 us -> 19.1 us  [on_device(): lax.all_to_all(gathered_block, 'row', split_axis=0, concat_axis=1, tiled=...]
  transfers between devices with their start and end apart: 22 -> 24, of which waited for: 22 -> 22; matrix products, arithmetic and copies ran while one was open for 4% -> 5% of each run, Pallas kernels for 0% -> 0%
where the time goes in v1:
time: 530 us; the launch traced here: 529 us
  waiting for transfers between devices  344 us (65%)
  starting transfers between devices  98.6 us (19%)
  local copies, waits for them, and re-layouts  45.3 us (9%)
  matrix products  15 us (3%)
  between operations  13.3 us (3%)
  blocking collectives  8.4 us (2%)
    ppermute x15, waiting for transfers between devices, passed_along(): lax.ppermute(value, axis, [(source, source + steps) for source in range(i...  128 us
    ppermute x15, starting transfers between devices, passed_along(): lax.ppermute(value, axis, [(source, source + steps) for source in range(i...  91.4 us
    all_gather x1, waiting for transfers between devices, on_device(): lax.all_gather(w_query, 'row', axis=0, tiled=True)  69.5 us
    all_gather x1, waiting for transfers between devices, on_device(): heads_block = lax.all_gather(heads_out, 'row', axis=0, tiled=True)  66.1 us
    reduce_scatter x1, waiting for transfers between devices, on_device(): lax.psum_scatter(jnp.dot(heads_block, w_output, preferred_element_type=jn...  28.2 us
    all_to_all x1, waiting for transfers between devices, on_device(): lax.all_to_all(gathered_block, 'row', split_axis=0, concat_axis=1, tiled=...  19.1 us
    all_gather x1, waiting for transfers between devices, on_device(): lax.all_gather(w_value, 'row', axis=0, tiled=True)  16.8 us
    ppermute x2, waiting for transfers between devices, trace_slabs(): lax.ppermute(newest[-1] if newest else payload, along_axis, pile)  14.2 us
  transfers between devices with their start and end apart: 24, of which 22 were waited for; matrix products, arithmetic and copies ran while one was open for 5% of the time, Pallas kernels for 0%

profile of v1, /device:TPU:2, one launch (start us, length us, event | category | flops | bytes accessed | tf_op | source)
XLA Modules:
  0.0 529.0 jit_solution(1086600263759001113)
XLA Ops:
  12.1 6.1 %collective-permute-done.1 = bf16[128,1024]{1,0:T(8,128)(2,1)S(1)} collective-permute-done((bf16[128,1024]{1,0:T(8,128)(2,1)S(1)}, bf16[128,1024]{1,0:T(8,128)(2,1)S(1)}, u32[]{:S(2)}, u32[]{:S(2)}) %collective-permute-start.1) | collective-permute-done | bytes 262176 | tf_op jit(solution)/shard_map/ppermute | solution.py:31
  18.5 8.1 %collective-permute-done.2 = bf16[128,1024]{1,0:T(8,128)(2,1)S(1)} collective-permute-done((bf16[128,1024]{1,0:T(8,128)(2,1)S(1)}, bf16[128,1024]{1,0:T(8,128)(2,1)S(1)}, u32[]{:S(2)}, u32[]{:S(2)}) %collective-permute-start.2) | collective-permute-done | bytes 262176 | tf_op jit(solution)/shard_map/ppermute | solution.py:31
  30.2 3.5 all-to-all-start
  34.8 19.1 %all-to-all-done = bf16[4,128,1024]{2,1,0:T(8,128)(2,1)S(1)} async-done(((bf16[4,128,1024]{2,1,0:T(8,128)(2,1)}), bf16[4,128,1024]{2,1,0:T(8,128)(2,1)S(1)}, u32[]{:S(2)}, u32[]{:S(2)}) %all-to-all-start) | async-done | bytes 1048608 | tf_op jit(solution)/shard_map/all_to_all | solution.py:83
  58.6 2.3 copy.45
  60.9 4.1 copy.20
  65.0 2.4 fusion.24
  67.6 16.8 %all-gather.7.cloned.1.call-done = bf16[4096,256]{1,0:T(8,128)(2,1)} async-done(((bf16[1024,256]{1,0:T(8,128)(2,1)}), bf16[4096,256]{1,0:T(8,128)(2,1)}) %all-gather.7.cloned.1.call-update) | async-done | bytes 2097168 | tf_op jit(solution)/shard_map/all_gather | solution.py:98
  84.4 2.4 convolution_convert_fusion.1
  86.8 8.4 %all_gather.17 = bf16[512,512]{1,0:T(8,128)(2,1)} all-gather(bf16[128,512]{1,0:T(8,128)(2,1)S(1)} %pad_maximum_fusion.1), channel_id=1, replica_groups=mesh['seq'=16,'row'=4,'col'=4] {'row'}, dimensions={0}, use_global_device_ids=true | all-gather | bytes 655360 | tf_op jit(solution)/shard_map/all_gather | solution.py:154
  95.2 2.1 copy.27
  101.6 69.5 %all-gather.9.cloned.1.call-done = bf16[4096,1024]{1,0:T(8,128)(2,1)} async-done(((bf16[1024,1024]{1,0:T(8,128)(2,1)}), bf16[4096,1024]{1,0:T(8,128)(2,1)}) %all-gather.9.cloned.1.call-update) | async-done | bytes 8388624 | tf_op jit(solution)/shard_map/all_gather | solution.py:88
  171.1 11.8 %copy.22 = bf16[1024,4096]{1,0:T(8,128)(2,1)} copy(bf16[1024,4096]{0,1:T(8,128)(2,1)} %bitcast.65) | data formatting | bytes 16777216 | tf_op jit(solution)/shard_map/dot_general | solution.py:86
  183.0 5.7 %fusion.25 = f32[128,8,128]{0,2,1:T(8,128)S(1)} fusion(bf16[128,4096,1]{1,0,2:T(8,128)(2,1)S(1)} %reshape.118, bf16[8,128,4096]{2,1,0:T(8,128)(2,1)} %bitcast.60), kind=kOutput, calls=%fused_computation.55 | convolution fusion | flops 1073741824 | bytes 9961472 | tf_op jit(solution)/shard_map/dot_general | solution.py:86
  191.2 232.4 %while.21 = (s32[]{:T(128)}, f32[2,4,128]{2,1,0:T(4,128)S(1)}, f32[2,4,128]{2,1,0:T(4,128)S(1)}, f32[2,4,128,128]{3,2,1,0:T(8,128)S(1)}, bf16[512,512]{0,1:T(8,1...) while((s32[]{:T(128)}, f32[2,4,128]{2,1,0:T(4,128)S(1)}, ...), condition=%wide.region_7.8_spmd, body=%wide.region_2.7_spmd.sunk | while | flops 272893952 | bytes 12386684 | solution.py:162
  191.2 3.5 collective-permute-start
  194.7 12.5 %collective-permute-done = bf16[512,512]{0,1:T(8,128)(2,1)S(1)} collective-permute-done((bf16[512,512]{0,1:T(8,128)(2,1)}, bf16[512,512]{0,1:T(8,128)(2,1)S(1)}, u32[]{:S(2)}, u32[]{:S(2)}) %collective-permute-start) | collective-permute-done | bytes 524320 | tf_op jit(solution)/shard_map/while/body/eval_jaxpr/ppermute | solution.py:50
  208.1 6.0 %collective-permute-start = (bf16[512,512]{0,1:T(8,128)(2,1)}, bf16[512,512]{0,1:T(8,128)(2,1)S(1)}, u32[]{:S(2)}, u32[]{:S(2)}) collective-permute-start(bf16[512,512]{0,1:T(8,128)(2,1)} %get-tuple-element.346), channel_id=1, source_target_pairs={{0,16},{16,32},{32,48},{48,64},{64,80},{80,96},{96,112},{112,128},... | collective-permute-start | bytes 1572872 | tf_op jit(solution)/shard_map/while/body/eval_jaxpr/ppermute | solution.py:50
  214.1 11.7 %collective-permute-done = bf16[512,512]{0,1:T(8,128)(2,1)S(1)} collective-permute-done((bf16[512,512]{0,1:T(8,128)(2,1)}, bf16[512,512]{0,1:T(8,128)(2,1)S(1)}, u32[]{:S(2)}, u32[]{:S(2)}) %collective-permute-start) | collective-permute-done | bytes 524320 | tf_op jit(solution)/shard_map/while/body/eval_jaxpr/ppermute | solution.py:50
  226.6 4.3 collective-permute-start
  231.0 10.8 %collective-permute-done = bf16[512,512]{0,1:T(8,128)(2,1)S(1)} collective-permute-done((bf16[512,512]{0,1:T(8,128)(2,1)}, bf16[512,512]{0,1:T(8,128)(2,1)S(1)}, u32[]{:S(2)}, u32[]{:S(2)}) %collective-permute-start) | collective-permute-done | bytes 524320 | tf_op jit(solution)/shard_map/while/body/eval_jaxpr/ppermute | solution.py:50
  242.6 5.2 collective-permute-start
  247.8 10.0 %collective-permute-done = bf16[512,512]{0,1:T(8,128)(2,1)S(1)} collective-permute-done((bf16[512,512]{0,1:T(8,128)(2,1)}, bf16[512,512]{0,1:T(8,128)(2,1)S(1)}, u32[]{:S(2)}, u32[]{:S(2)}) %collective-permute-start) | collective-permute-done | bytes 524320 | tf_op jit(solution)/shard_map/while/body/eval_jaxpr/ppermute | solution.py:50
  258.7 5.1 collective-permute-start
  263.8 9.1 %collective-permute-done = bf16[512,512]{0,1:T(8,128)(2,1)S(1)} collective-permute-done((bf16[512,512]{0,1:T(8,128)(2,1)}, bf16[512,512]{0,1:T(8,128)(2,1)S(1)}, u32[]{:S(2)}, u32[]{:S(2)}) %collective-permute-start) | collective-permute-done | bytes 524320 | tf_op jit(solution)/shard_map/while/body/eval_jaxpr/ppermute | solution.py:50
  273.7 7.2 %collective-permute-start = (bf16[512,512]{0,1:T(8,128)(2,1)}, bf16[512,512]{0,1:T(8,128)(2,1)S(1)}, u32[]{:S(2)}, u32[]{:S(2)}) collective-permute-start(bf16[512,512]{0,1:T(8,128)(2,1)} %get-tuple-element.346), channel_id=1, source_target_pairs={{0,16},{16,32},{32,48},{48,64},{64,80},{80,96},{96,112},{112,128},... | collective-permute-start | bytes 1572872 | tf_op jit(solution)/shard_map/while/body/eval_jaxpr/ppermute | solution.py:50
  281.0 8.3 %collective-permute-done = bf16[512,512]{0,1:T(8,128)(2,1)S(1)} collective-permute-done((bf16[512,512]{0,1:T(8,128)(2,1)}, bf16[512,512]{0,1:T(8,128)(2,1)S(1)}, u32[]{:S(2)}, u32[]{:S(2)}) %collective-permute-start) | collective-permute-done | bytes 524320 | tf_op jit(solution)/shard_map/while/body/eval_jaxpr/ppermute | solution.py:50
  290.1 5.5 %collective-permute-start = (bf16[512,512]{0,1:T(8,128)(2,1)}, bf16[512,512]{0,1:T(8,128)(2,1)S(1)}, u32[]{:S(2)}, u32[]{:S(2)}) collective-permute-start(bf16[512,512]{0,1:T(8,128)(2,1)} %get-tuple-element.346), channel_id=1, source_target_pairs={{0,16},{16,32},{32,48},{48,64},{64,80},{80,96},{96,112},{112,128},... | collective-permute-start | bytes 1572872 | tf_op jit(solution)/shard_map/while/body/eval_jaxpr/ppermute | solution.py:50
  295.7 7.4 %collective-permute-done = bf16[512,512]{0,1:T(8,128)(2,1)S(1)} collective-permute-done((bf16[512,512]{0,1:T(8,128)(2,1)}, bf16[512,512]{0,1:T(8,128)(2,1)S(1)}, u32[]{:S(2)}, u32[]{:S(2)}) %collective-permute-start) | collective-permute-done | bytes 524320 | tf_op jit(solution)/shard_map/while/body/eval_jaxpr/ppermute | solution.py:50
  303.9 7.2 %collective-permute-start = (bf16[512,512]{0,1:T(8,128)(2,1)}, bf16[512,512]{0,1:T(8,128)(2,1)S(1)}, u32[]{:S(2)}, u32[]{:S(2)}) collective-permute-start(bf16[512,512]{0,1:T(8,128)(2,1)} %get-tuple-element.346), channel_id=1, source_target_pairs={{0,16},{16,32},{32,48},{48,64},{64,80},{80,96},{96,112},{112,128},... | collective-permute-start | bytes 1572872 | tf_op jit(solution)/shard_map/while/body/eval_jaxpr/ppermute | solution.py:50
  311.2 6.9 %collective-permute-done = bf16[512,512]{0,1:T(8,128)(2,1)S(1)} collective-permute-done((bf16[512,512]{0,1:T(8,128)(2,1)}, bf16[512,512]{0,1:T(8,128)(2,1)S(1)}, u32[]{:S(2)}, u32[]{:S(2)}) %collective-permute-start) | collective-permute-done | bytes 524320 | tf_op jit(solution)/shard_map/while/body/eval_jaxpr/ppermute | solution.py:50
  319.0 5.5 %collective-permute-start = (bf16[512,512]{0,1:T(8,128)(2,1)}, bf16[512,512]{0,1:T(8,128)(2,1)S(1)}, u32[]{:S(2)}, u32[]{:S(2)}) collective-permute-start(bf16[512,512]{0,1:T(8,128)(2,1)} %get-tuple-element.346), channel_id=1, source_target_pairs={{0,16},{16,32},{32,48},{48,64},{64,80},{80,96},{96,112},{112,128},... | collective-permute-start | bytes 1572872 | tf_op jit(solution)/shard_map/while/body/eval_jaxpr/ppermute | solution.py:50
  324.5 6.9 %collective-permute-done = bf16[512,512]{0,1:T(8,128)(2,1)S(1)} collective-permute-done((bf16[512,512]{0,1:T(8,128)(2,1)}, bf16[512,512]{0,1:T(8,128)(2,1)S(1)}, u32[]{:S(2)}, u32[]{:S(2)}) %collective-permute-start) | collective-permute-done | bytes 524320 | tf_op jit(solution)/shard_map/while/body/eval_jaxpr/ppermute | solution.py:50
  332.3 5.5 %collective-permute-start = (bf16[512,512]{0,1:T(8,128)(2,1)}, bf16[512,512]{0,1:T(8,128)(2,1)S(1)}, u32[]{:S(2)}, u32[]{:S(2)}) collective-permute-start(bf16[512,512]{0,1:T(8,128)(2,1)} %get-tuple-element.346), channel_id=1, source_target_pairs={{0,16},{16,32},{32,48},{48,64},{64,80},{80,96},{96,112},{112,128},... | collective-permute-start | bytes 1572872 | tf_op jit(solution)/shard_map/while/body/eval_jaxpr/ppermute | solution.py:50
  337.8 7.8 %collective-permute-done = bf16[512,512]{0,1:T(8,128)(2,1)S(1)} collective-permute-done((bf16[512,512]{0,1:T(8,128)(2,1)}, bf16[512,512]{0,1:T(8,128)(2,1)S(1)}, u32[]{:S(2)}, u32[]{:S(2)}) %collective-permute-start) | collective-permute-done | bytes 524320 | tf_op jit(solution)/shard_map/while/body/eval_jaxpr/ppermute | solution.py:50
  346.4 4.7 collective-permute-start
  351.1 6.9 %collective-permute-done = bf16[512,512]{0,1:T(8,128)(2,1)S(1)} collective-permute-done((bf16[512,512]{0,1:T(8,128)(2,1)}, bf16[512,512]{0,1:T(8,128)(2,1)S(1)}, u32[]{:S(2)}, u32[]{:S(2)}) %collective-permute-start) | collective-permute-done | bytes 524320 | tf_op jit(solution)/shard_map/while/body/eval_jaxpr/ppermute | solution.py:50
  358.9 7.7 %collective-permute-start = (bf16[512,512]{0,1:T(8,128)(2,1)}, bf16[512,512]{0,1:T(8,128)(2,1)S(1)}, u32[]{:S(2)}, u32[]{:S(2)}) collective-permute-start(bf16[512,512]{0,1:T(8,128)(2,1)} %get-tuple-element.346), channel_id=1, source_target_pairs={{0,16},{16,32},{32,48},{48,64},{64,80},{80,96},{96,112},{112,128},... | collective-permute-start | bytes 1572872 | tf_op jit(solution)/shard_map/while/body/eval_jaxpr/ppermute | solution.py:50
  366.6 7.1 %collective-permute-done = bf16[512,512]{0,1:T(8,128)(2,1)S(1)} collective-permute-done((bf16[512,512]{0,1:T(8,128)(2,1)}, bf16[512,512]{0,1:T(8,128)(2,1)S(1)}, u32[]{:S(2)}, u32[]{:S(2)}) %collective-permute-start) | collective-permute-done | bytes 524320 | tf_op jit(solution)/shard_map/while/body/eval_jaxpr/ppermute | solution.py:50
  374.5 7.8 %collective-permute-start = (bf16[512,512]{0,1:T(8,128)(2,1)}, bf16[512,512]{0,1:T(8,128)(2,1)S(1)}, u32[]{:S(2)}, u32[]{:S(2)}) collective-permute-start(bf16[512,512]{0,1:T(8,128)(2,1)} %get-tuple-element.346), channel_id=1, source_target_pairs={{0,16},{16,32},{32,48},{48,64},{64,80},{80,96},{96,112},{112,128},... | collective-permute-start | bytes 1572872 | tf_op jit(solution)/shard_map/while/body/eval_jaxpr/ppermute | solution.py:50
  382.3 6.9 %collective-permute-done = bf16[512,512]{0,1:T(8,128)(2,1)S(1)} collective-permute-done((bf16[512,512]{0,1:T(8,128)(2,1)}, bf16[512,512]{0,1:T(8,128)(2,1)S(1)}, u32[]{:S(2)}, u32[]{:S(2)}) %collective-permute-start) | collective-permute-done | bytes 524320 | tf_op jit(solution)/shard_map/while/body/eval_jaxpr/ppermute | solution.py:50
  390.1 10.7 %collective-permute-start = (bf16[512,512]{0,1:T(8,128)(2,1)}, bf16[512,512]{0,1:T(8,128)(2,1)S(1)}, u32[]{:S(2)}, u32[]{:S(2)}) collective-permute-start(bf16[512,512]{0,1:T(8,128)(2,1)} %get-tuple-element.346), channel_id=1, source_target_pairs={{0,16},{16,32},{32,48},{48,64},{64,80},{80,96},{96,112},{112,128},... | collective-permute-start | bytes 1572872 | tf_op jit(solution)/shard_map/while/body/eval_jaxpr/ppermute | solution.py:50
  400.8 8.7 %collective-permute-done = bf16[512,512]{0,1:T(8,128)(2,1)S(1)} collective-permute-done((bf16[512,512]{0,1:T(8,128)(2,1)}, bf16[512,512]{0,1:T(8,128)(2,1)S(1)}, u32[]{:S(2)}, u32[]{:S(2)}) %collective-permute-start) | collective-permute-done | bytes 524320 | tf_op jit(solution)/shard_map/while/body/eval_jaxpr/ppermute | solution.py:50
  410.4 5.5 %collective-permute-start = (bf16[512,512]{0,1:T(8,128)(2,1)}, bf16[512,512]{0,1:T(8,128)(2,1)S(1)}, u32[]{:S(2)}, u32[]{:S(2)}) collective-permute-start(bf16[512,512]{0,1:T(8,128)(2,1)} %get-tuple-element.346), channel_id=1, source_target_pairs={{0,16},{16,32},{32,48},{48,64},{64,80},{80,96},{96,112},{112,128},... | collective-permute-start | bytes 1572872 | tf_op jit(solution)/shard_map/while/body/eval_jaxpr/ppermute | solution.py:50
  415.9 6.9 %collective-permute-done = bf16[512,512]{0,1:T(8,128)(2,1)S(1)} collective-permute-done((bf16[512,512]{0,1:T(8,128)(2,1)}, bf16[512,512]{0,1:T(8,128)(2,1)S(1)}, u32[]{:S(2)}, u32[]{:S(2)}) %collective-permute-start) | collective-permute-done | bytes 524320 | tf_op jit(solution)/shard_map/while/body/eval_jaxpr/ppermute | solution.py:50
  424.7 66.1 %all-gather.11.cloned.1.call-done = bf16[512,1024]{0,1:T(8,128)(2,1)} async-done(((bf16[128,1024]{0,1:T(8,128)(2,1)}), bf16[512,1024]{0,1:T(8,128)(2,1)}) %all-gather.11.cloned.1.call-update) | async-done | bytes 1048592 | tf_op jit(solution)/shard_map/all_gather | solution.py:165
  490.8 3.5 convolution_convert_fusion
  494.3 28.2 %reduce-scatter.2.cloned.1.call-done = bf16[128,1024]{1,0:T(8,128)(2,1)} async-done(((bf16[512,1024]{1,0:T(8,128)(2,1)}), bf16[128,1024]{1,0:T(8,128)(2,1)}) %reduce-scatter.2.cloned.1.call-update) | async-done | bytes 262160 | tf_op jit(solution)/shard_map/reduce_scatter | solution.py:166
  (92 shorter events, 35.5 us)
Async XLA Ops:
  6.5 484.3 %copy-start = (bf16[1024,1024]{1,0:T(8,128)(2,1)S(1)}, bf16[1024,1024]{1,0:T(8,128)(2,1)}, u32[]{:S(2)}) copy-start(bf16[1024,1024]{1,0:T(8,128)(2,1)} %param.13) | copy-start | bytes 6291460
  6.5 2.2 copy-start.4
  6.5 54.4 %all-gather.5.cloned.1.call-start = ((), (), s32[]{:S(2)}) async-start(), calls=%async_computation.2 | async-start | bytes 2621440 | tf_op jit(solution)/shard_map/all_gather | solution.py:93
  7.3 77.2 %all-gather.7.cloned.1.call-start = ((), (), s32[]{:S(2)}) async-start(), calls=%async_computation.3 | async-start | bytes 2621440 | tf_op jit(solution)/shard_map/all_gather | solution.py:98
  8.0 163.1 %all-gather.9.cloned.1.call-start = ((), (), s32[]{:S(2)}) async-start(), calls=%async_computation.4 | async-start | bytes 10485760 | tf_op jit(solution)/shard_map/all_gather | solution.py:88
  8.8 9.4 %collective-permute-start.1 = (bf16[128,1024]{1,0:T(8,128)(2,1)S(1)}, bf16[128,1024]{1,0:T(8,128)(2,1)S(1)}, u32[]{:S(2)}, u32[]{:S(2)}) collective-permute-start(bf16[128,1024]{1,0:T(8,128)(2,1)S(1)} %copy-done.4), channel_id=1, source_target_pairs={{0,1},{1,2},{2,3},{3,0},{4,5},{5,6},{6,7},{7,4},{8,9},{9,10},{10,1... | collective-permute-start | bytes 786440 | tf_op jit(solution)/shard_map/ppermute | solution.py:31
  10.4 8.1 %collective-permute-start.3 = (bf16[128,1024]{1,0:T(8,128)(2,1)S(1)}, bf16[128,1024]{1,0:T(8,128)(2,1)S(1)}, u32[]{:S(2)}, u32[]{:S(2)}) collective-permute-start(bf16[128,1024]{1,0:T(8,128)(2,1)S(1)} %copy-done.4), channel_id=1, source_target_pairs={{1,0},{2,1},{3,2},{0,3},{5,4},{6,5},{7,6},{4,7},{9,8},{10,9},{11,1... | collective-permute-start | bytes 786440 | tf_op jit(solution)/shard_map/ppermute | solution.py:34
  18.2 8.5 %copy-start.5 = (bf16[128,1024]{1,0:T(8,128)(2,1)}, bf16[128,1024]{1,0:T(8,128)(2,1)S(1)}, u32[]{:S(2)}) copy-start(bf16[128,1024]{1,0:T(8,128)(2,1)S(1)} %collective-permute-done.1) | copy-start | bytes 786436
  18.2 8.5 %collective-permute-start.2 = (bf16[128,1024]{1,0:T(8,128)(2,1)S(1)}, bf16[128,1024]{1,0:T(8,128)(2,1)S(1)}, u32[]{:S(2)}, u32[]{:S(2)}) collective-permute-start(bf16[128,1024]{1,0:T(8,128)(2,1)S(1)} %collective-permute-done.1), channel_id=1, source_target_pairs={{0,1},{1,2},{2,3},{3,0},{4,5},{5,6},{6,7},{7,4},{8,9},{9,10},{10,1... | collective-permute-start | bytes 786440 | tf_op jit(solution)/shard_map/ppermute | solution.py:31
  18.5 8.1 %copy-start.6 = (bf16[128,1024]{1,0:T(8,128)(2,1)}, bf16[128,1024]{1,0:T(8,128)(2,1)S(1)}, u32[]{:S(2)}) copy-start(bf16[128,1024]{1,0:T(8,128)(2,1)S(1)} %collective-permute-done.3) | copy-start | bytes 786436
  26.6 0.7 copy-start.7
  30.2 23.7 %all-to-all-start = ((bf16[4,128,1024]{2,1,0:T(8,128)(2,1)}), bf16[4,128,1024]{2,1,0:T(8,128)(2,1)S(1)}, u32[]{:S(2)}, u32[]{:S(2)}) async-start(bf16[4,128,1024]{2,1,0:T(8,128)(2,1)} %gather_fusion), calls=%async_computation | async-start | bytes 2097152 | tf_op jit(solution)/shard_map/all_to_all | solution.py:83
  33.7 457.1 %all-gather.11.cloned.1.call-start = ((), (), s32[]{:S(2)}) async-start(), calls=%async_computation.5 | async-start | bytes 1310720 | tf_op jit(solution)/shard_map/all_gather | solution.py:165
  54.0 1.0 copy-start.1
  188.7 1.0 copy-start.3
  188.7 0.9 copy-start.8
  189.6 1.0 copy-start.2
  191.2 16.0 %collective-permute-start = (bf16[512,512]{0,1:T(8,128)(2,1)}, bf16[512,512]{0,1:T(8,128)(2,1)S(1)}, u32[]{:S(2)}, u32[]{:S(2)}) collective-permute-start(bf16[512,512]{0,1:T(8,128)(2,1)} %get-tuple-element.346), channel_id=1, source_target_pairs={{0,16},{16,32},{32,48},{48,64},{64,80},{80,96},{96,112},{112,128},... | collective-permute-start | bytes 1572872 | tf_op jit(solution)/shard_map/while/body/eval_jaxpr/ppermute | solution.py:50
  208.1 17.7 %collective-permute-start = (bf16[512,512]{0,1:T(8,128)(2,1)}, bf16[512,512]{0,1:T(8,128)(2,1)S(1)}, u32[]{:S(2)}, u32[]{:S(2)}) collective-permute-start(bf16[512,512]{0,1:T(8,128)(2,1)} %get-tuple-element.346), channel_id=1, source_target_pairs={{0,16},{16,32},{32,48},{48,64},{64,80},{80,96},{96,112},{112,128},... | collective-permute-start | bytes 1572872 | tf_op jit(solution)/shard_map/while/body/eval_jaxpr/ppermute | solution.py:50
  226.6 15.2 %collective-permute-start = (bf16[512,512]{0,1:T(8,128)(2,1)}, bf16[512,512]{0,1:T(8,128)(2,1)S(1)}, u32[]{:S(2)}, u32[]{:S(2)}) collective-permute-start(bf16[512,512]{0,1:T(8,128)(2,1)} %get-tuple-element.346), channel_id=1, source_target_pairs={{0,16},{16,32},{32,48},{48,64},{64,80},{80,96},{96,112},{112,128},... | collective-permute-start | bytes 1572872 | tf_op jit(solution)/shard_map/while/body/eval_jaxpr/ppermute | solution.py:50
  242.6 15.2 %collective-permute-start = (bf16[512,512]{0,1:T(8,128)(2,1)}, bf16[512,512]{0,1:T(8,128)(2,1)S(1)}, u32[]{:S(2)}, u32[]{:S(2)}) collective-permute-start(bf16[512,512]{0,1:T(8,128)(2,1)} %get-tuple-element.346), channel_id=1, source_target_pairs={{0,16},{16,32},{32,48},{48,64},{64,80},{80,96},{96,112},{112,128},... | collective-permute-start | bytes 1572872 | tf_op jit(solution)/shard_map/while/body/eval_jaxpr/ppermute | solution.py:50
  258.7 14.3 %collective-permute-start = (bf16[512,512]{0,1:T(8,128)(2,1)}, bf16[512,512]{0,1:T(8,128)(2,1)S(1)}, u32[]{:S(2)}, u32[]{:S(2)}) collective-permute-start(bf16[512,512]{0,1:T(8,128)(2,1)} %get-tuple-element.346), channel_id=1, source_target_pairs={{0,16},{16,32},{32,48},{48,64},{64,80},{80,96},{96,112},{112,128},... | collective-permute-start | bytes 1572872 | tf_op jit(solution)/shard_map/while/body/eval_jaxpr/ppermute | solution.py:50
  273.7 15.5 %collective-permute-start = (bf16[512,512]{0,1:T(8,128)(2,1)}, bf16[512,512]{0,1:T(8,128)(2,1)S(1)}, u32[]{:S(2)}, u32[]{:S(2)}) collective-permute-start(bf16[512,512]{0,1:T(8,128)(2,1)} %get-tuple-element.346), channel_id=1, source_target_pairs={{0,16},{16,32},{32,48},{48,64},{64,80},{80,96},{96,112},{112,128},... | collective-permute-start | bytes 1572872 | tf_op jit(solution)/shard_map/while/body/eval_jaxpr/ppermute | solution.py:50
  290.1 13.0 %collective-permute-start = (bf16[512,512]{0,1:T(8,128)(2,1)}, bf16[512,512]{0,1:T(8,128)(2,1)S(1)}, u32[]{:S(2)}, u32[]{:S(2)}) collective-permute-start(bf16[512,512]{0,1:T(8,128)(2,1)} %get-tuple-element.346), channel_id=1, source_target_pairs={{0,16},{16,32},{32,48},{48,64},{64,80},{80,96},{96,112},{112,128},... | collective-permute-start | bytes 1572872 | tf_op jit(solution)/shard_map/while/body/eval_jaxpr/ppermute | solution.py:50
  303.9 14.2 %collective-permute-start = (bf16[512,512]{0,1:T(8,128)(2,1)}, bf16[512,512]{0,1:T(8,128)(2,1)S(1)}, u32[]{:S(2)}, u32[]{:S(2)}) collective-permute-start(bf16[512,512]{0,1:T(8,128)(2,1)} %get-tuple-element.346), channel_id=1, source_target_pairs={{0,16},{16,32},{32,48},{48,64},{64,80},{80,96},{96,112},{112,128},... | collective-permute-start | bytes 1572872 | tf_op jit(solution)/shard_map/while/body/eval_jaxpr/ppermute | solution.py:50
  319.0 12.5 %collective-permute-start = (bf16[512,512]{0,1:T(8,128)(2,1)}, bf16[512,512]{0,1:T(8,128)(2,1)S(1)}, u32[]{:S(2)}, u32[]{:S(2)}) collective-permute-start(bf16[512,512]{0,1:T(8,128)(2,1)} %get-tuple-element.346), channel_id=1, source_target_pairs={{0,16},{16,32},{32,48},{48,64},{64,80},{80,96},{96,112},{112,128},... | collective-permute-start | bytes 1572872 | tf_op jit(solution)/shard_map/while/body/eval_jaxpr/ppermute | solution.py:50
  332.3 13.3 %collective-permute-start = (bf16[512,512]{0,1:T(8,128)(2,1)}, bf16[512,512]{0,1:T(8,128)(2,1)S(1)}, u32[]{:S(2)}, u32[]{:S(2)}) collective-permute-start(bf16[512,512]{0,1:T(8,128)(2,1)} %get-tuple-element.346), channel_id=1, source_target_pairs={{0,16},{16,32},{32,48},{48,64},{64,80},{80,96},{96,112},{112,128},... | collective-permute-start | bytes 1572872 | tf_op jit(solution)/shard_map/while/body/eval_jaxpr/ppermute | solution.py:50
  346.4 11.6 %collective-permute-start = (bf16[512,512]{0,1:T(8,128)(2,1)}, bf16[512,512]{0,1:T(8,128)(2,1)S(1)}, u32[]{:S(2)}, u32[]{:S(2)}) collective-permute-start(bf16[512,512]{0,1:T(8,128)(2,1)} %get-tuple-element.346), channel_id=1, source_target_pairs={{0,16},{16,32},{32,48},{48,64},{64,80},{80,96},{96,112},{112,128},... | collective-permute-start | bytes 1572872 | tf_op jit(solution)/shard_map/while/body/eval_jaxpr/ppermute | solution.py:50
  358.9 14.8 %collective-permute-start = (bf16[512,512]{0,1:T(8,128)(2,1)}, bf16[512,512]{0,1:T(8,128)(2,1)S(1)}, u32[]{:S(2)}, u32[]{:S(2)}) collective-permute-start(bf16[512,512]{0,1:T(8,128)(2,1)} %get-tuple-element.346), channel_id=1, source_target_pairs={{0,16},{16,32},{32,48},{48,64},{64,80},{80,96},{96,112},{112,128},... | collective-permute-start | bytes 1572872 | tf_op jit(solution)/shard_map/while/body/eval_jaxpr/ppermute | solution.py:50
  374.5 14.8 %collective-permute-start = (bf16[512,512]{0,1:T(8,128)(2,1)}, bf16[512,512]{0,1:T(8,128)(2,1)S(1)}, u32[]{:S(2)}, u32[]{:S(2)}) collective-permute-start(bf16[512,512]{0,1:T(8,128)(2,1)} %get-tuple-element.346), channel_id=1, source_target_pairs={{0,16},{16,32},{32,48},{48,64},{64,80},{80,96},{96,112},{112,128},... | collective-permute-start | bytes 1572872 | tf_op jit(solution)/shard_map/while/body/eval_jaxpr/ppermute | solution.py:50
  390.1 19.4 %collective-permute-start = (bf16[512,512]{0,1:T(8,128)(2,1)}, bf16[512,512]{0,1:T(8,128)(2,1)S(1)}, u32[]{:S(2)}, u32[]{:S(2)}) collective-permute-start(bf16[512,512]{0,1:T(8,128)(2,1)} %get-tuple-element.346), channel_id=1, source_target_pairs={{0,16},{16,32},{32,48},{48,64},{64,80},{80,96},{96,112},{112,128},... | collective-permute-start | bytes 1572872 | tf_op jit(solution)/shard_map/while/body/eval_jaxpr/ppermute | solution.py:50
  410.4 12.4 %collective-permute-start = (bf16[512,512]{0,1:T(8,128)(2,1)}, bf16[512,512]{0,1:T(8,128)(2,1)S(1)}, u32[]{:S(2)}, u32[]{:S(2)}) collective-permute-start(bf16[512,512]{0,1:T(8,128)(2,1)} %get-tuple-element.346), channel_id=1, source_target_pairs={{0,16},{16,32},{32,48},{48,64},{64,80},{80,96},{96,112},{112,128},... | collective-permute-start | bytes 1572872 | tf_op jit(solution)/shard_map/while/body/eval_jaxpr/ppermute | solution.py:50
  424.6 97.8 %reduce-scatter.2.cloned.1.call-start = ((), (), s32[]{:S(2)}) async-start(), calls=%async_computation.6 | async-start | bytes 1310720 | tf_op jit(solution)/shard_map/reduce_scatter | solution.py:166
Sparse Core Ops, SparseCore 0:
  9.1 40.8 all-gather.4
  51.9 32.5 all-gather.6
  86.3 84.8 all-gather.8
  424.7 66.0 all-gather.10
  494.4 28.0 reduce-scatter.1
